TPU v7x, 128 devices: a whole 4x4x4 slice. The times are simulated.
128 devices in a mesh: rows: 8 (over y, z_lo), pairs: 16 (over z_hi, x, core).
Axes of the slice: x: 4, y: 4, z: 4 (z_hi: 2, z_lo: 2; z = z_hi * 2 + z_lo), core: 2. Of those that a mesh axis runs over, the one named last changes fastest.
Arguments:
- unit_rows: float32 [8, 16, 192, 8192], P('rows', 'pairs'), may hold values from -6 to 6
- unit_counts: int32 [8, 16], P('rows'), may hold values from 1 to 192, 1024 in all within a row
- seating: int32 [32], replicated, may hold values from 0 to 31, each once
- channel_scale: float32 [8192], replicated, may hold values from 0.25 to 4
Outputs:
- rotated: float32 [8192, 8192], P('rows', 'pairs')
Inputs may be any that keep to these rules, and one draw needn't show every extreme that they name: `unit_counts`: each row of 16 counts sums to 1024, and in each row the largest is exactly 192. `seating`: each block once.
All inputs are finite; a program needn't handle non-finite values.
Results may differ from a plain program's by a relative error of at most 0.0001.
Values sent between devices are 32-bit elements; how exact they have to be, the bound alone decides.
No kernel may reach another device: no remote copies, remote signals or barrier semaphores. Data moves between devices by JAX's collectives and lax.ppermute only.
A program may use at most 128 MiB of HBM per device.

v0:
```python
import jax
import jax.numpy as jnp
from jax import lax
from jax.sharding import PartitionSpec as P

ROWS_DEV = 1024
BLOCK = 256
ROUNDS = 2


epsilon = 1e-06


def passed_along(array, axis, by):
    length = lax.axis_size(axis)
    pairs = [(i, i + by) for i in range(length) if 0 <= i + by < length]
    return lax.ppermute(array, axis, pairs)


def rotate(panels):
    partial_gram = lax.dot_general(
        panels,
        panels,
        (((0,), (0,)), ((), ())),
        precision=lax.Precision.HIGHEST,
        preferred_element_type=jnp.float32,
    )
    gram_full = lax.psum(partial_gram, "rows")
    diag_terms = jnp.diagonal(gram_full)
    skew_part = (
        gram_full
        * (diag_terms[None, :] - diag_terms[:, None])
        / (2.0 * (diag_terms[:, None] ** 2 + diag_terms[None, :] ** 2) + epsilon)
    )
    skew_square = jnp.dot(skew_part, skew_part, precision=lax.Precision.HIGHEST)
    identity = jnp.eye(skew_part.shape[0], dtype=jnp.float32)
    numerator = identity + skew_part + 0.25 * skew_square
    sym_part = identity - 0.25 * skew_square
    factor = jnp.linalg.cholesky(sym_part)
    transposed = jax.scipy.linalg.cho_solve((factor, True), numerator.T)
    return jnp.dot(panels, transposed.T, precision=lax.Precision.HIGHEST)


def advance(panels):
    half_width = panels.shape[1] // 2
    upper = panels[:, :half_width]
    lower = panels[:, half_width:]
    pair_index = lax.axis_index("pairs")
    last_pair = lax.axis_size("pairs") - 1
    upward = jnp.where(pair_index == 0, lower, upper)
    came_up = passed_along(upward, "pairs", 1)
    came_down = passed_along(lower, "pairs", -1)
    new_upper = jnp.where(pair_index == 0, upper, came_up)
    new_lower = jnp.where(pair_index == last_pair, upper, came_down)
    return jnp.concatenate([new_upper, new_lower], axis=1)


def compact(panels, group_counts, capacity):
    unit_ends = jnp.cumsum(group_counts)
    target = lax.iota(jnp.int32, ROWS_DEV)
    passed = (target[:, None] >= unit_ends[None, :]).astype(jnp.int32)
    owner_unit = jnp.sum(passed, axis=1)
    owner_start = jnp.sum(passed * group_counts[None, :], axis=1)
    source = owner_unit * capacity + target - owner_start
    return jnp.take(panels, source, axis=0)


def local(unit_rows, unit_counts, seating, channel_scale):
    capacity = unit_rows.shape[2]
    columns = unit_rows.shape[3]
    group_counts = unit_counts[0]
    pair_index = lax.axis_index("pairs")
    slot_ids = lax.iota(jnp.int32, group_counts.shape[0])
    own_count = jnp.sum(jnp.where(slot_ids == pair_index, group_counts, 0))
    live_rows = (lax.iota(jnp.int32, capacity) < own_count)[:, None]
    scaled = jnp.where(live_rows, unit_rows[0, 0] * channel_scale[None, :], 0.0)
    seated = jnp.take(scaled.reshape(capacity, columns // BLOCK, BLOCK), seating, axis=1).reshape(
        capacity, columns
    )
    panels = lax.all_to_all(seated, "pairs", split_axis=1, concat_axis=0, tiled=True)
    current = panels
    for round_index in range(ROUNDS):
        current = rotate(current)
        if round_index + 1 < ROUNDS:
            current = advance(current)
    current = compact(current, group_counts, capacity)
    return current


def solution(mesh):
    return jax.shard_map(
        local,
        mesh=mesh,
        in_specs=(P("rows", "pairs", None, None), P("rows", None), P(), P()),
        out_specs=P("rows", "pairs"),
        check_vma=False,
    )
```

profile of v0, /device:TPU:3, one launch (start us, length us, event | category | flops | bytes accessed | tf_op | source)
XLA Modules:
  0.0 755.0 jit_solution(14425828180244923408)
XLA Ops:
  9.8 7.8 %copy.47 = f32[24,8,32,256]{3,2,1,0:T(8,128)} copy(f32[24,8,32,256]{3,1,2,0:T(8,128)} %bitcast.147) | data formatting | bytes 12582912
  17.7 9.5 %fusion.2 = f32[192,32,256]{2,0,1:T(8,128)} fusion(f32[192,32,256]{2,1,0:T(8,128)} %bitcast.144, f32[32,256]{1,0:T(8,128)S(1)} %mul.64, pred[192]{0:T(512)(128)(4,1)S(1)} %iota_compare_fusion.5), kind=kLoop, calls=%fused_computation.13 | loop fusion | flops 3145728 | bytes 12615872 | tf_op jit(solution)/shard_map/jit(_where)/select_n | solution.py:76
  27.2 6.4 gather_fusion
  33.6 9.1 %copy.33 = f32[192,32,256]{2,1,0:T(8,128)} copy(f32[192,32,256]{2,0,1:T(8,128)} %bitcast.145) | data formatting | bytes 12582912 | tf_op jit(solution)/shard_map/jit(_take)/gather | solution.py:77
  42.6 7.7 %gather.22 = f32[192,16,512]{2,1,0:T(8,128)} reshape(f32[192,32,256]{2,1,0:T(8,128)} %copy.33) | data formatting | bytes 12582912 | tf_op jit(solution)/shard_map/jit(_take)/gather | solution.py:77
  50.5 6.8 copy_select_fusion
  57.3 79.6 %all_to_all.16 = f32[192,16,512]{2,0,1:T(8,128)S(1)} all-to-all(f32[192,16,512]{2,0,1:T(8,128)S(1)} %copy_select_fusion), channel_id=1, replica_groups=mesh['rows'=8,'pairs'=16] {'pairs'}, dimensions={1} | all-to-all | bytes 12582912 | tf_op jit(solution)/shard_map/all_to_all | solution.py:80
  136.9 2.7 copy-done.1
  139.6 11.4 %fusion.5 = f32[512,512]{0,1:T(8,128)} fusion(f32[192,16,512]{2,0,1:T(8,128)S(1)} %all_to_all.16), kind=kOutput, calls=%fused_computation.23 | convolution fusion | flops 9663676416 | bytes 7340032 | tf_op jit(solution)/shard_map/dot_general | solution.py:21
  151.1 72.8 %all-reduce.4.cloned.1.call-done = f32[512,512]{0,1:T(8,128)} async-done(((f32[512,512]{0,1:T(8,128)}), f32[512,512]{0,1:T(8,128)}) %all-reduce.4.cloned.1.call-update) | async-done | bytes 1048592 | tf_op jit(solution)/shard_map/psum | solution.py:28
  223.9 9.0 %gather_fusion.1 = f32[512]{0:T(512)S(1)} fusion(f32[512,512]{0,1:T(8,128)} %all-reduce.4.cloned.1.call-done, s32[512]{0:T(512)S(1)} %bitcast.142), kind=kCustom, calls=%fused_computation.1 | custom fusion | bytes 8192 | tf_op jit(solution)/shard_map/jit(diagonal)/cond/branch_0_fun/gather | solution.py:29
  232.9 4.1 convolution_multiply_fusion.1
  237.0 1.4 convert_subtract_fusion.1
  240.0 11.7 %cholesky.286 = f32[128,128]{1,0:T(8,128)S(1)} custom-call(f32[128,128]{1,0:T(8,128)S(1)} %cholesky.426), custom_call_target="Cholesky" | custom-call | tf_op jit(solution)/shard_map/jit(cholesky)/cholesky | solution.py:39
  251.7 9.8 %custom-call.33 = f32[1,128,128]{1,2,0:T(8,128)S(1)} custom-call(f32[1,128,128]{2,1,0:T(8,128)S(1)} %get-tuple-element.72), custom_call_target="InvertDiagBlocksLowerTriangular" | custom-call | tf_op jit(solution)/shard_map/jit(cholesky)/cholesky | solution.py:39
  264.2 11.9 %cholesky.305 = f32[128,128]{1,0:T(8,128)S(1)} custom-call(f32[128,128]{1,0:T(8,128)S(1)} %cholesky.430), custom_call_target="Cholesky" | custom-call | tf_op jit(solution)/shard_map/jit(cholesky)/cholesky | solution.py:39
  276.1 9.8 %custom-call.34 = f32[1,128,128]{1,2,0:T(8,128)S(1)} custom-call(f32[1,128,128]{2,1,0:T(8,128)S(1)} %get-tuple-element.69), custom_call_target="InvertDiagBlocksLowerTriangular" | custom-call | tf_op jit(solution)/shard_map/jit(cholesky)/cholesky | solution.py:39
  287.5 11.7 %cholesky.326 = f32[128,128]{1,0:T(8,128)S(1)} custom-call(f32[128,128]{1,0:T(8,128)S(1)} %cholesky.435), custom_call_target="Cholesky" | custom-call | tf_op jit(solution)/shard_map/jit(cholesky)/cholesky | solution.py:39
  299.9 9.8 %custom-call.35 = f32[1,128,128]{1,2,0:T(8,128)S(1)} custom-call(f32[1,128,128]{2,1,0:T(8,128)S(1)} %get-tuple-element.66), custom_call_target="InvertDiagBlocksLowerTriangular" | custom-call | tf_op jit(solution)/shard_map/jit(cholesky)/cholesky | solution.py:39
  311.1 11.9 %cholesky.343 = f32[128,128]{1,0:T(8,128)S(1)} custom-call(f32[128,128]{1,0:T(8,128)S(1)} %convolution_subtract_fusion.17), custom_call_target="Cholesky" | custom-call | tf_op jit(solution)/shard_map/jit(cholesky)/cholesky | solution.py:39
  327.0 7.8 %while.4 = (s32[]{:T(128)}, f32[512,512]{1,0:T(8,128)S(1)}, s32[4,2]{0,1:T(2,128)S(1)}, f32[4,128,128]{2,1,0:T(8,128)S(1)}, s32[]{:T(128)}) while((s32[]{:T(128)}, f32[512,512]{1,0:T(8,128)S(1)}, s32[4,2]{0,1:T(2,128)S(1)}, f32[4,128,128]{2,1,0:T(8,128)S(1)}, s32[]{:T(128)}) %tuple.56), condition=%wide.while_cond, body=%wide.while_body.sunk | while | flops 2 | bytes 131181 | solution.py:40
  327.6 1.3 bitcast_dynamic-update-slice_fusion.4
  334.8 39.3 %custom-call.36 = f32[4,128,128]{1,2,0:T(8,128)S(1)} custom-call(f32[4,128,128]{2,1,0:T(8,128)S(1)} %get-tuple-element.21), custom_call_target="InvertDiagBlocksLowerTriangular" | custom-call | tf_op jit(solution)/shard_map/jit(_cho_solve)/triangular_solve | solution.py:40
  380.4 13.0 %fusion.12 = f32[3072,512]{0,1:T(8,128)S(1)} fusion(f32[3072,512]{1,0:T(8,128)} %bitcast.146, f32[128,512]{1,0:T(8,128)S(1)} %fusion.104, f32[128,512]{1,0:T(8,128)S(1)} %fusion.102, f32[128,512]{1,0:T(8,128)S(1)} %fusion.100, f32[128,512]{1,0:T(8,128)S(1)} %fusion.99), kind=kOutput, calls=%fused_computation.54 | convolution fusion | flops 9664462848 | bytes 13631488 | tf_op jit(solution)/shard_map/dot_general | solution.py:41
  393.4 2.5 slice_select_fusion.2
  397.0 8.0 %collective-permute-start = (f32[3072,256]{0,1:T(8,128)}, f32[3072,256]{0,1:T(8,128)}, u32[]{:S(2)}, u32[]{:S(2)}) collective-permute-start(f32[3072,256]{0,1:T(8,128)} %get-tuple-element.47), channel_id=1, source_target_pairs={{0,1},{1,2},{2,3},{3,4},{4,5},{5,6},{6,7},{7,8},{8,9},{9,10},{10,1... | collective-permute-start | bytes 9437192 | tf_op jit(solution)/shard_map/ppermute | solution.py:17
  405.1 1.9 collective-permute-start.1
  407.0 32.6 %collective-permute-done = f32[3072,256]{0,1:T(8,128)} collective-permute-done((f32[3072,256]{0,1:T(8,128)}, f32[3072,256]{0,1:T(8,128)}, u32[]{:S(2)}, u32[]{:S(2)}) %collective-permute-start) | collective-permute-done | bytes 3145760 | tf_op jit(solution)/shard_map/ppermute | solution.py:17
  439.6 4.2 collective-permute-done.1
  443.8 4.5 slice_select_fusion.1
  448.3 1.6 copy-done.2
  450.0 11.7 %fusion.4 = f32[512,512]{0,1:T(8,128)} fusion(f32[3072,256]{0,1:T(8,128)S(1)} %get-tuple-element.46, f32[3072,256]{0,1:T(8,128)S(1)} %get-tuple-element.45), kind=kOutput, calls=%fused_computation.15 | convolution fusion | flops 9665249280 | bytes 7340032 | tf_op jit(solution)/shard_map/dot_general | solution.py:21
  462.1 74.6 %all-reduce.6.cloned.1.call-done = f32[512,512]{0,1:T(8,128)} async-done(((f32[512,512]{0,1:T(8,128)}), f32[512,512]{0,1:T(8,128)}) %all-reduce.6.cloned.1.call-update) | async-done | bytes 1048592 | tf_op jit(solution)/shard_map/psum | solution.py:28
  536.8 8.7 %gather_fusion.2 = f32[512]{0:T(512)S(1)} fusion(f32[512,512]{0,1:T(8,128)} %all-reduce.6.cloned.1.call-done, s32[512]{0:T(512)S(1)} %bitcast.143), kind=kCustom, calls=%fused_computation.2 | custom fusion | bytes 8192 | tf_op jit(solution)/shard_map/jit(diagonal)/cond/branch_0_fun/gather | solution.py:29
  545.5 4.0 convolution_multiply_fusion
  549.5 1.8 convert_subtract_fusion
  551.3 2.6 copy.40
  553.9 1.8 fusion.27
  556.6 11.7 %cholesky.358 = f32[128,128]{1,0:T(8,128)S(1)} custom-call(f32[128,128]{1,0:T(8,128)S(1)} %cholesky.439), custom_call_target="Cholesky" | custom-call | tf_op jit(solution)/shard_map/jit(cholesky)/cholesky | solution.py:39
  569.5 9.8 %custom-call.37 = f32[1,128,128]{1,2,0:T(8,128)S(1)} custom-call(f32[1,128,128]{2,1,0:T(8,128)S(1)} %get-tuple-element.62), custom_call_target="InvertDiagBlocksLowerTriangular" | custom-call | tf_op jit(solution)/shard_map/jit(cholesky)/cholesky | solution.py:39
  579.3 1.9 constant_dynamic-update-slice_fusion.3
  582.5 11.9 %cholesky.377 = f32[128,128]{1,0:T(8,128)S(1)} custom-call(f32[128,128]{1,0:T(8,128)S(1)} %cholesky.443), custom_call_target="Cholesky" | custom-call | tf_op jit(solution)/shard_map/jit(cholesky)/cholesky | solution.py:39
  596.4 9.8 %custom-call.38 = f32[1,128,128]{1,2,0:T(8,128)S(1)} custom-call(f32[1,128,128]{2,1,0:T(8,128)S(1)} %get-tuple-element.59), custom_call_target="InvertDiagBlocksLowerTriangular" | custom-call | tf_op jit(solution)/shard_map/jit(cholesky)/cholesky | solution.py:39
  607.1 1.4 convolution_subtract_fusion.14
  608.6 11.7 %cholesky.398 = f32[128,128]{1,0:T(8,128)S(1)} custom-call(f32[128,128]{1,0:T(8,128)S(1)} %cholesky.448), custom_call_target="Cholesky" | custom-call | tf_op jit(solution)/shard_map/jit(cholesky)/cholesky | solution.py:39
  621.6 9.8 %custom-call.39 = f32[1,128,128]{1,2,0:T(8,128)S(1)} custom-call(f32[1,128,128]{2,1,0:T(8,128)S(1)} %get-tuple-element.56), custom_call_target="InvertDiagBlocksLowerTriangular" | custom-call | tf_op jit(solution)/shard_map/jit(cholesky)/cholesky | solution.py:39
  632.3 1.4 convolution_subtract_fusion.16
  633.7 12.1 %cholesky.415 = f32[128,128]{1,0:T(8,128)S(1)} custom-call(f32[128,128]{1,0:T(8,128)S(1)} %convolution_subtract_fusion.16), custom_call_target="Cholesky" | custom-call | tf_op jit(solution)/shard_map/jit(cholesky)/cholesky | solution.py:39
  649.7 2.3 select_select_fusion
  652.0 11.4 %while.5 = (s32[]{:T(128)}, f32[512,512]{1,0:T(8,128)}, s32[4,2]{0,1:T(2,128)S(1)}, f32[4,128,128]{2,1,0:T(8,128)S(1)}, s32[]{:T(128)}) while((s32[]{:T(128)}, f32[512,512]{1,0:T(8,128)}, s32[4,2]{0,1:T(2,128)S(1)}, f32[4,128,128]{2,1,0:T(8,128)S(1)}, s32[]{:T(128)}) %tuple.66), condition=%wide.while_cond.clone, body=%wide.while_body.clone.sunk | while | flops 2 | bytes 131181 | solution.py:40
  652.7 2.2 bitcast_dynamic-update-slice_fusion.5
  655.5 2.2 bitcast_dynamic-update-slice_fusion.5
  658.4 2.2 bitcast_dynamic-update-slice_fusion.5
  661.3 2.2 bitcast_dynamic-update-slice_fusion.5
  664.1 40.1 %custom-call.40 = f32[4,128,128]{1,2,0:T(8,128)S(1)} custom-call(f32[4,128,128]{2,1,0:T(8,128)} %copy-done.10), custom_call_target="InvertDiagBlocksLowerTriangular" | custom-call | tf_op jit(solution)/shard_map/jit(_cho_solve)/triangular_solve | solution.py:40
  704.3 1.5 fusion.61
  705.8 1.4 convolution_subtract_fusion.3
  707.6 1.4 convolution_subtract_fusion.2
  709.5 1.7 convolution_subtract_fusion.9
  713.6 1.4 convolution_subtract_fusion
  715.4 1.6 convolution_subtract_fusion.8
  717.3 22.3 %fusion.3 = f32[3072,512]{1,0:T(8,128)} fusion(f32[3072,256]{0,1:T(8,128)S(1)} %copy-done.3, f32[3072,256]{0,1:T(8,128)S(1)} %get-tuple-element.45, f32[128,512]{1,0:T(8,128)S(1)} %fusion.111, f32[128,512]{1,0:T(8,128)S(1)} %fusion.109, f32[128,512]{1,0:T(8,128)S(1)} %fusion.107, f32[128,512]{1,0:T(8,128)S(1)} %fusion.106), kind=kOutput, calls=%fused_computation.14 | convolution fusion | flops 9666035712 | bytes 13631488 | tf_op jit(solution)/shard_map/dot_general | solution.py:41
  739.6 6.8 gather_fusion.3
  746.4 1.5 broadcast_select_fusion
  (128 shorter events, 44.0 us)
Async XLA Ops:
  6.5 217.4 %all-reduce.4.cloned.1.call-start = ((), (), s32[]{:S(2)}) async-start(), calls=%async_computation.1 | async-start | bytes 2097152 | tf_op jit(solution)/shard_map/psum | solution.py:28
  9.8 7.8 %copy-start.11 = (f32[8192]{0:T(1024)S(1)}, f32[8192]{0:T(1024)}, u32[]{:S(2)}) copy-start(f32[8192]{0:T(1024)} %param.10) | copy-start | bytes 98308
  136.9 2.7 copy-start.1
  151.1 385.7 %all-reduce.6.cloned.1.call-start = ((), (), s32[]{:S(2)}) async-start(), calls=%async_computation.2 | async-start | bytes 2097152 | tf_op jit(solution)/shard_map/psum | solution.py:28
  223.9 13.0 %copy-start.5 = (f32[512,512]{0,1:T(8,128)S(1)}, f32[512,512]{0,1:T(8,128)}, u32[]{:S(2)}) copy-start(f32[512,512]{0,1:T(8,128)} %all-reduce.4.cloned.1.call-done) | copy-start | bytes 3145732
  238.7 135.4 %copy-start.7 = (f32[512,512]{1,0:T(8,128)S(1)}, f32[512,512]{1,0:T(8,128)}, u32[]{:S(2)}) copy-start(f32[512,512]{1,0:T(8,128)} %get-tuple-element.52) | copy-start | bytes 3145732
  239.0 1.0 copy-start.9
  393.4 3.6 copy-start
  397.0 42.6 %collective-permute-start = (f32[3072,256]{0,1:T(8,128)}, f32[3072,256]{0,1:T(8,128)}, u32[]{:S(2)}, u32[]{:S(2)}) collective-permute-start(f32[3072,256]{0,1:T(8,128)} %get-tuple-element.47), channel_id=1, source_target_pairs={{0,1},{1,2},{2,3},{3,4},{4,5},{5,6},{6,7},{7,8},{8,9},{9,10},{10,1... | collective-permute-start | bytes 9437192 | tf_op jit(solution)/shard_map/ppermute | solution.py:17
  405.1 38.7 %collective-permute-start.1 = (f32[3072,256]{0,1:T(8,128)S(1)}, f32[3072,256]{0,1:T(8,128)}, u32[]{:S(2)}, u32[]{:S(2)}) collective-permute-start(f32[3072,256]{0,1:T(8,128)S(1)} %get-tuple-element.48), channel_id=1, source_target_pairs={{1,0},{2,1},{3,2},{4,3},{5,4},{6,5},{7,6},{8,7},{9,8},{10,9},{11,1... | collective-permute-start | bytes 9437192 | tf_op jit(solution)/shard_map/ppermute | solution.py:17
  448.3 1.7 copy-start.2
  448.3 13.4 %copy-start.12 = (s32[1,16]{1,0:T(1,128)S(1)}, s32[1,16]{1,0:T(1,128)}, u32[]{:S(2)}) copy-start(s32[1,16]{1,0:T(1,128)} %param.8) | copy-start | bytes 196
  545.5 4.0 copy-start.4
  549.5 1.8 copy-start.6
  555.6 1.0 copy-start.8
  663.4 0.7 copy-start.10
  704.2 13.1 %copy-start.3 = (f32[3072,256]{0,1:T(8,128)S(1)}, f32[3072,256]{0,1:T(8,128)}, u32[]{:S(2)}) copy-start(f32[3072,256]{0,1:T(8,128)} %copy-done.2) | copy-start | bytes 9437188
Sparse Core Ops, SparseCore 0:
  151.2 72.7 all-reduce.3
  461.8 74.8 all-reduce.5
where the time goes:
time: 769 us; the launch traced here: 755 us
  other arithmetic  276 us (36%)
  waiting for transfers between devices  184 us (24%)
  matrix products  98.8 us (13%)
  local copies, waits for them, and re-layouts  86.9 us (11%)
  blocking collectives  79.6 us (10%)
  between operations  19.4 us (3%)
  starting transfers between devices  10 us (1%)
    another operation x29, other arithmetic, rotate(): factor = jnp.linalg.cholesky(sym_part)  160 us
    psum x2, waiting for transfers between devices, rotate(): gram_full = lax.psum(partial_gram, 'rows')  147 us
    another operation x5, other arithmetic, rotate(): transposed = jax.scipy.linalg.cho_solve((factor, True), numerator.T)  81.9 us
    all_to_all x1, blocking collectives, local(): lax.all_to_all(seated, 'pairs', split_axis=1, concat_axis=0, tiled=True)  79.6 us
    ppermute x2, waiting for transfers between devices, passed_along(): return lax.ppermute(array, axis, pairs)  36.8 us
    dot_general x2, matrix products, rotate(): return jnp.dot(panels, transposed.T, precision=lax.Precision.HIGHEST)  35.3 us
    dot_general x2, matrix products, rotate(): lax.dot_general(panels, panels, (((0,), (0,)), ((), ())), precision=lax.P...  23.2 us
    gather x3, local copies, waits for them, and re-layouts, local(): jnp.take(scaled.reshape(capacity, columns // BLOCK, BLOCK), seating, axis=1)  23.1 us
  transfers between devices with their start and end apart: 4, of which 4 were waited for; matrix products, arithmetic and copies ran while one was open for 0% of the time, Pallas kernels for 0%

commit v1 on v0

--- a/solution.py
+++ b/solution.py
@@ -7,8 +7,10 @@
 BLOCK = 256
 ROUNDS = 2
 
-
 epsilon = 1e-06
+HI = lax.Precision.HIGHEST
+NEWTON_TOL_SQ = 1e-4
+NEWTON_MAX = 60
 
 
 def passed_along(array, axis, by):
@@ -17,12 +19,38 @@
     return lax.ppermute(array, axis, pairs)
 
 
+def spd_inverse(sym_part):
+    n = sym_part.shape[0]
+    identity = jnp.eye(n, dtype=jnp.float32)
+    bound = jnp.max(jnp.sum(jnp.abs(sym_part), axis=1))
+    scale = 2.0 / (1.0 + bound)
+    inverse = scale * identity
+    residual = identity - scale * sym_part
+
+    def cond(state):
+        step, _, _, err = state
+        return jnp.logical_and(err > NEWTON_TOL_SQ, step < NEWTON_MAX)
+
+    def body(state):
+        step, inverse, residual, _ = state
+        inverse = inverse + jnp.dot(inverse, residual, precision=HI)
+        residual = identity - jnp.dot(sym_part, inverse, precision=HI)
+        return step + 1, inverse, residual, jnp.sum(residual * residual)
+
+    state = (jnp.int32(0), inverse, residual, jnp.sum(residual * residual))
+    _, inverse, residual, _ = lax.while_loop(cond, body, state)
+    inverse = inverse + jnp.dot(inverse, residual, precision=HI)
+    residual = identity - jnp.dot(sym_part, inverse, precision=HI)
+    inverse = inverse + jnp.dot(inverse, residual, precision=HI)
+    return inverse
+
+
 def rotate(panels):
     partial_gram = lax.dot_general(
         panels,
         panels,
         (((0,), (0,)), ((), ())),
-        precision=lax.Precision.HIGHEST,
+        precision=HI,
         preferred_element_type=jnp.float32,
     )
     gram_full = lax.psum(partial_gram, "rows")
@@ -32,13 +60,12 @@
         * (diag_terms[None, :] - diag_terms[:, None])
         / (2.0 * (diag_terms[:, None] ** 2 + diag_terms[None, :] ** 2) + epsilon)
     )
-    skew_square = jnp.dot(skew_part, skew_part, precision=lax.Precision.HIGHEST)
+    skew_square = jnp.dot(skew_part, skew_part, precision=HI)
     identity = jnp.eye(skew_part.shape[0], dtype=jnp.float32)
     numerator = identity + skew_part + 0.25 * skew_square
     sym_part = identity - 0.25 * skew_square
-    factor = jnp.linalg.cholesky(sym_part)
-    transposed = jax.scipy.linalg.cho_solve((factor, True), numerator.T)
-    return jnp.dot(panels, transposed.T, precision=lax.Precision.HIGHEST)
+    rotation = jnp.dot(numerator, spd_inverse(sym_part), precision=HI)
+    return jnp.dot(panels, rotation, precision=HI)
 
 
 def advance(panels):
@@ -69,21 +96,16 @@
     capacity = unit_rows.shape[2]
     columns = unit_rows.shape[3]
     group_counts = unit_counts[0]
-    pair_index = lax.axis_index("pairs")
-    slot_ids = lax.iota(jnp.int32, group_counts.shape[0])
-    own_count = jnp.sum(jnp.where(slot_ids == pair_index, group_counts, 0))
-    live_rows = (lax.iota(jnp.int32, capacity) < own_count)[:, None]
-    scaled = jnp.where(live_rows, unit_rows[0, 0] * channel_scale[None, :], 0.0)
+    scaled = unit_rows[0, 0] * channel_scale[None, :]
     seated = jnp.take(scaled.reshape(capacity, columns // BLOCK, BLOCK), seating, axis=1).reshape(
         capacity, columns
     )
     panels = lax.all_to_all(seated, "pairs", split_axis=1, concat_axis=0, tiled=True)
-    current = panels
+    current = compact(panels, group_counts, capacity)
     for round_index in range(ROUNDS):
         current = rotate(current)
         if round_index + 1 < ROUNDS:
             current = advance(current)
-    current = compact(current, group_counts, capacity)
     return current
 
 

time: 769 us -> 499 us (0.65)
  the two profiles are of different devices: /device:TPU:3 before, /device:TPU:2 now
where the time goes in v1:
time: 499 us; the launch traced here: 490 us
  waiting for transfers between devices  256 us (51%)
  matrix products  105 us (21%)
  local copies, waits for them, and re-layouts  67 us (13%)
  other arithmetic  22.6 us (5%)
  between operations  15.6 us (3%)
  starting transfers between devices  14.1 us (3%)
  loops' own time  8.89 us (2%)
    psum x2, waiting for transfers between devices, rotate(): gram_full = lax.psum(partial_gram, 'rows')  159 us
    all_to_all x1, waiting for transfers between devices, local(): lax.all_to_all(seated, 'pairs', split_axis=1, concat_axis=0, tiled=True)  84.9 us
    dot_general x11, matrix products, body(): residual = identity - jnp.dot(sym_part, inverse, precision=HI)  45.7 us
    gather x3, local copies, waits for them, and re-layouts, local(): jnp.take(scaled.reshape(capacity, columns // BLOCK, BLOCK), seating, axis=1)  23.2 us
    dot_general x11, matrix products, body(): inverse = inverse + jnp.dot(inverse, residual, precision=HI)  20.5 us
    gather x2, local copies, waits for them, and re-layouts, rotate(): diag_terms = jnp.diagonal(gram_full)  17.4 us
    unnamed x36, local copies, waits for them, and re-layouts  12.3 us
    ppermute x2, waiting for transfers between devices, passed_along(): return lax.ppermute(array, axis, pairs)  12.1 us
  transfers between devices with their start and end apart: 5, of which 5 were waited for; matrix products, arithmetic and copies ran while one was open for 0% of the time, Pallas kernels for 0%

profile of v1, /device:TPU:2, one launch (start us, length us, event | category | flops | bytes accessed | tf_op | source)
XLA Modules:
  0.0 489.8 jit_solution(11899552848003923042)
XLA Ops:
  7.9 7.8 %copy.44 = f32[24,8,32,256]{3,2,1,0:T(8,128)} copy(f32[24,8,32,256]{3,1,2,0:T(8,128)} %bitcast.66) | data formatting | bytes 12582912
  15.7 9.1 %copy_multiply_fusion = f32[192,32,256]{2,0,1:T(8,128)} fusion(f32[192,32,256]{2,1,0:T(8,128)} %bitcast.64, f32[32,256]{1,0:T(8,128)S(1)} %mul.96), kind=kLoop, calls=%fused_computation.16 | loop fusion | flops 1572864 | bytes 12615680 | tf_op jit(solution)/shard_map/mul | solution.py:99
  24.8 6.4 %gather_fusion = f32[32,192,256]{2,1,0:T(8,128)} fusion(f32[192,32,256]{2,0,1:T(8,128)} %copy_multiply_fusion, s32[1024]{0:T(1024)S(1)} %pad_clamp_fusion), kind=kCustom, calls=%fused_computation | custom fusion | bytes 12583040 | tf_op jit(solution)/shard_map/jit(_take)/gather | solution.py:100
  31.2 9.1 %copy.35 = f32[192,32,256]{2,1,0:T(8,128)} copy(f32[192,32,256]{2,0,1:T(8,128)} %bitcast.65) | data formatting | bytes 12582912 | tf_op jit(solution)/shard_map/jit(_take)/gather | solution.py:100
  40.3 7.7 %gather.18 = f32[192,16,512]{2,1,0:T(8,128)} reshape(f32[192,32,256]{2,1,0:T(8,128)} %copy.35) | data formatting | bytes 12582912 | tf_op jit(solution)/shard_map/jit(_take)/gather | solution.py:100
  48.2 3.6 broadcast_select_fusion
  51.8 6.3 %copy.36 = f32[192,16,512]{2,0,1:T(8,128)} copy(f32[192,16,512]{2,1,0:T(8,128)S(1)} %broadcast_select_fusion) | data formatting | bytes 12582912 | tf_op jit(solution)/shard_map/jit(_take)/select_n | solution.py:100
  58.1 8.3 %all-to-all-start = ((f32[192,16,512]{2,0,1:T(8,128)}), f32[192,16,512]{2,0,1:T(8,128)}, u32[]{:S(2)}, u32[]{:S(2)}) async-start(f32[192,16,512]{2,0,1:T(8,128)} %copy.36), calls=%async_computation | async-start | bytes 12582912 | tf_op jit(solution)/shard_map/all_to_all | solution.py:103
  66.8 84.9 %all-to-all-done = f32[192,16,512]{2,0,1:T(8,128)} async-done(((f32[192,16,512]{2,0,1:T(8,128)}), f32[192,16,512]{2,0,1:T(8,128)}, u32[]{:S(2)}, u32[]{:S(2)}) %all-to-all-start) | async-done | bytes 6291488 | tf_op jit(solution)/shard_map/all_to_all | solution.py:103
  151.7 6.8 %gather_fusion.1 = f32[1024,512]{1,0:T(8,128)S(1)} fusion(f32[3072,512]{1,0:T(8,128)} %bitcast.4, s32[1024]{0:T(1024)S(1)} %broadcast_clamp_fusion), kind=kCustom, calls=%fused_computation.1 | custom fusion | bytes 4198400 | tf_op jit(solution)/shard_map/jit(_take)/gather | solution.py:92
  158.6 5.2 %fusion.8 = f32[512,512]{1,0:T(8,128)} fusion(f32[1024,512]{1,0:T(8,128)S(1)} %gather_fusion.1, pred[1024]{0:T(1024)(128)(4,1)S(1)} %compare_and_fusion), kind=kOutput, calls=%fused_computation.29 | convolution fusion | flops 3221749760 | bytes 3146752 | tf_op jit(solution)/shard_map/dot_general | solution.py:49
  163.9 77.8 %all-reduce.3.cloned.1.call-done = f32[512,512]{1,0:T(8,128)} async-done(((f32[512,512]{1,0:T(8,128)}), f32[512,512]{1,0:T(8,128)}) %all-reduce.3.cloned.1.call-update) | async-done | bytes 1048592 | tf_op jit(solution)/shard_map/psum | solution.py:56
  241.7 8.8 %gather_fusion.2 = f32[512]{0:T(512)S(1)} fusion(f32[512,512]{1,0:T(8,128)} %all-reduce.3.cloned.1.call-done, s32[512]{0:T(512)S(1)} %bitcast.62), kind=kCustom, calls=%fused_computation.2 | custom fusion | bytes 8192 | tf_op jit(solution)/shard_map/jit(diagonal)/cond/branch_0_fun/gather | solution.py:57
  250.5 2.5 convert_subtract_fusion.5
  254.4 1.9 multiply_reduce_fusion.3
  256.3 1.6 copy.38
  257.9 34.8 %while.30 = (s32[]{:T(128)}, f32[512,512]{1,0:T(8,128)S(1)}, f32[512,512]{0,1:T(8,128)S(1)}, f32[]{:T(128)}, f32[512,512]{1,0:T(8,128)S(1)}, /*index=5*/s32[]{:T(128)}) while((s32[]{:T(128)}, f32[512,512]{1,0:T(8,128)S(1)}, f32[512,512]{0,1:T(8,128)S(1)}, f32[]{:T(128)}, f32[512,512]{1,0:T(8,128)S(1)}, /*index=5*/s32[]{:T(128)}) %tuple.63), condition=%wide.region_9.10_spmd.clone, body=%wide.region_7.9_spmd.clone.sunk | while | flops 3222798336 | bytes 8388693 | solution.py:41
  258.6 1.9 convolution_add_fusion.8
  260.5 4.2 multiply_reduce_fusion.6
  265.4 1.9 convolution_add_fusion.8
  267.3 4.2 multiply_reduce_fusion.6
  272.2 1.9 convolution_add_fusion.8
  274.1 4.2 multiply_reduce_fusion.6
  279.0 1.9 convolution_add_fusion.8
  280.9 4.2 multiply_reduce_fusion.6
  285.8 1.9 convolution_add_fusion.8
  287.7 4.2 multiply_reduce_fusion.6
  292.7 1.9 convolution_add_fusion.5
  294.6 1.9 convert_subtract_fusion.2
  296.5 1.9 convolution_add_fusion.4
  298.4 2.2 fusion.13
  300.6 3.9 fusion.6
  304.5 1.2 slice_select_fusion.2
  305.7 1.9 collective-permute-start
  307.6 3.9 collective-permute-start.1
  311.4 10.6 %collective-permute-done = f32[1024,256]{0,1:T(8,128)} collective-permute-done((f32[1024,256]{0,1:T(8,128)}, f32[1024,256]{0,1:T(8,128)}, u32[]{:S(2)}, u32[]{:S(2)}) %collective-permute-start) | collective-permute-done | bytes 1048608 | tf_op jit(solution)/shard_map/ppermute | solution.py:19
  322.1 1.4 collective-permute-done.1
  323.5 1.9 slice_select_fusion.1
  325.4 1.0 copy-done.6
  326.8 4.5 fusion.11
  331.3 81.5 %all-reduce.5.cloned.1.call-done = f32[512,512]{1,0:T(8,128)} async-done(((f32[512,512]{1,0:T(8,128)}), f32[512,512]{1,0:T(8,128)}) %all-reduce.5.cloned.1.call-update) | async-done | bytes 1048592 | tf_op jit(solution)/shard_map/psum | solution.py:56
  412.8 8.6 %gather_fusion.3 = f32[512]{0:T(512)S(1)} fusion(f32[512,512]{1,0:T(8,128)} %all-reduce.5.cloned.1.call-done, s32[512]{0:T(512)S(1)} %bitcast.63), kind=kCustom, calls=%fused_computation.3 | custom fusion | bytes 8192 | tf_op jit(solution)/shard_map/jit(diagonal)/cond/branch_0_fun/gather | solution.py:57
  421.4 2.5 convert_subtract_fusion.1
  423.9 0.7 reduce_max.19
  425.4 1.8 multiply_reduce_fusion.2
  427.2 1.6 copy.40
  428.8 41.0 %while.31 = (s32[]{:T(128)}, f32[512,512]{1,0:T(8,128)S(1)}, f32[512,512]{0,1:T(8,128)S(1)}, f32[]{:T(128)}, f32[512,512]{1,0:T(8,128)S(1)}, /*index=5*/s32[]{:T(128)}) while((s32[]{:T(128)}, f32[512,512]{1,0:T(8,128)S(1)}, f32[512,512]{0,1:T(8,128)S(1)}, f32[]{:T(128)}, f32[512,512]{1,0:T(8,128)S(1)}, ...), condition=%wide.region_16.17_spmd.clone, body=%wide.region_14.16_spmd.clone.sunk | while | flops 3222798336 | bytes 8388693 | solution.py:41
  429.5 1.9 convolution_add_fusion.9
  431.4 4.1 multiply_reduce_fusion.7
  436.2 1.9 convolution_add_fusion.9
  438.1 4.1 multiply_reduce_fusion.7
  442.9 1.9 convolution_add_fusion.9
  444.8 4.1 multiply_reduce_fusion.7
  449.6 1.9 convolution_add_fusion.9
  451.5 4.1 multiply_reduce_fusion.7
  456.3 1.9 convolution_add_fusion.9
  458.2 4.1 multiply_reduce_fusion.7
  463.0 1.9 convolution_add_fusion.9
  464.8 4.1 multiply_reduce_fusion.7
  469.9 1.9 convolution_add_fusion.3
  471.7 1.9 convert_subtract_fusion.3
  473.6 1.9 convolution_add_fusion.2
  475.5 2.2 fusion.16
  477.7 4.8 fusion.10
  (66 shorter events, 4.0 us)
Async XLA Ops:
  7.9 7.8 %copy-start.14 = (f32[8192]{0:T(1024)S(1)}, f32[8192]{0:T(1024)}, u32[]{:S(2)}) copy-start(f32[8192]{0:T(1024)} %param.11) | copy-start | bytes 98308
  58.0 8.3 %copy-start.15 = (s32[1,16]{1,0:T(1,128)S(1)}, s32[1,16]{1,0:T(1,128)}, u32[]{:S(2)}) copy-start(s32[1,16]{1,0:T(1,128)} %param.9) | copy-start | bytes 196
  58.1 93.7 %all-to-all-start = ((f32[192,16,512]{2,0,1:T(8,128)}), f32[192,16,512]{2,0,1:T(8,128)}, u32[]{:S(2)}, u32[]{:S(2)}) async-start(f32[192,16,512]{2,0,1:T(8,128)} %copy.36), calls=%async_computation | async-start | bytes 12582912 | tf_op jit(solution)/shard_map/all_to_all | solution.py:103
  66.3 175.3 %all-reduce.3.cloned.1.call-start = ((), (), s32[]{:S(2)}) async-start(), calls=%async_computation.1 | async-start | bytes 2097152 | tf_op jit(solution)/shard_map/psum | solution.py:56
  158.5 5.2 %copy-start = (f32[1024,512]{1,0:T(8,128)}, f32[1024,512]{1,0:T(8,128)S(1)}, u32[]{:S(2)}) copy-start(f32[1024,512]{1,0:T(8,128)S(1)} %gather_fusion.1) | copy-start | bytes 6291460
  163.8 249.0 %all-reduce.5.cloned.1.call-start = ((), (), s32[]{:S(2)}) async-start(), calls=%async_computation.2 | async-start | bytes 2097152 | tf_op jit(solution)/shard_map/psum | solution.py:56
  241.7 8.8 %copy-start.10 = (f32[512,512]{1,0:T(8,128)S(1)}, f32[512,512]{1,0:T(8,128)}, u32[]{:S(2)}) copy-start(f32[512,512]{1,0:T(8,128)} %all-reduce.3.cloned.1.call-done) | copy-start | bytes 3145732
  253.0 3.3 copy-start.2
  292.7 1.9 copy-start.3
  296.5 1.9 copy-start.11
  298.4 2.2 copy-start.1
  305.7 16.4 %collective-permute-start = (f32[1024,256]{0,1:T(8,128)}, f32[1024,256]{0,1:T(8,128)}, u32[]{:S(2)}, u32[]{:S(2)}) collective-permute-start(f32[1024,256]{0,1:T(8,128)} %get-tuple-element.181), channel_id=1, source_target_pairs={{0,1},{1,2},{2,3},{3,4},{4,5},{5,6},{6,7},{7,8},{8,9},{9,10},{10,1... | collective-permute-start | bytes 3145736 | tf_op jit(solution)/shard_map/ppermute | solution.py:19
  307.6 15.9 %collective-permute-start.1 = (f32[1024,256]{0,1:T(8,128)S(1)}, f32[1024,256]{0,1:T(8,128)}, u32[]{:S(2)}, u32[]{:S(2)}) collective-permute-start(f32[1024,256]{0,1:T(8,128)S(1)} %get-tuple-element.182), channel_id=1, source_target_pairs={{1,0},{2,1},{3,2},{4,3},{5,4},{6,5},{7,6},{8,7},{9,8},{10,9},{11,1... | collective-permute-start | bytes 3145736 | tf_op jit(solution)/shard_map/ppermute | solution.py:19
  325.4 1.0 copy-start.6
  325.4 1.4 copy-start.8
  412.8 8.6 %copy-start.12 = (f32[512,512]{1,0:T(8,128)S(1)}, f32[512,512]{1,0:T(8,128)}, u32[]{:S(2)}) copy-start(f32[512,512]{1,0:T(8,128)} %all-reduce.5.cloned.1.call-done) | copy-start | bytes 3145732
  423.9 3.3 copy-start.4
  469.8 1.9 copy-start.5
  473.6 1.9 copy-start.13
  475.5 2.2 copy-start.7
  475.5 2.2 copy-start.9
Sparse Core Ops, SparseCore 0:
  163.9 77.7 all-reduce.2
  331.4 81.3 all-reduce.4
